TPU v7x, 128 devices: a whole 4x4x4 slice. The times are simulated.
128 devices in a mesh: tile: 32 (over x_lo, y, z), src: 4 (over x_hi, core).
Axes of the slice: x: 4 (x_hi: 2, x_lo: 2; x = x_hi * 2 + x_lo), y: 4, z: 4, core: 2. Of those that a mesh axis runs over, the one named last changes fastest.
Arguments:
- tile_tokens: bfloat16 [32768, 2048], P(('tile', 'src')), may hold values from -6 to 6
- norm_gain: float32 [2048], replicated, may hold values from 0.25 to 2.5
- up_weight: bfloat16 [2048, 2816], P('tile'), may hold values from -0.125 to 0.125
- down_weight: bfloat16 [2816, 2048], P('tile'), may hold values from -0.109375 to 0.109375
- head_weight: bfloat16 [2048, 768], P(None, 'src'), may hold values from -0.125 to 0.125
- source_index: int32 [128, 2], replicated, may hold values from 0 to 96, as said below
- source_cutoff: int32 [128], replicated, may hold values from 8 to 16
- source_weight: float32 [128], replicated, may hold values from 0.3 to 3
Outputs:
- intensity: float32 [128, 4096], P(('tile', 'src'))
Inputs may be any that keep to these rules, and one draw needn't show every extreme that they name: `source_index`: in each aligned group of 4 source points the first has the least value of the group in both coordinates, the second lies exactly 32 beyond it in both, and every other lies within 32 of the first in both.
All inputs are finite; a program needn't handle non-finite values.
Results may differ from a plain program's by a relative error of at most 0.0007.
Values may be sent and summed in bfloat16 or wider, within the bound.
No kernel may reach another device: no remote copies, remote signals or barrier semaphores. Data moves between devices by JAX's collectives and lax.ppermute only.
A program may use at most 128 MiB of HBM per device.

v0:
```python
import math

import jax
import jax.numpy as jnp
from jax import lax
from jax.sharding import PartitionSpec as P

GRID = 16
SUB = 8
W = 32
REG = 64
PIX = 64
SRC_DEV = 4
PATCH = 256
ORD = 128


def dft_tables():
    frequency = jnp.arange(W, dtype=jnp.int32) - W // 2
    position = jnp.arange(PIX, dtype=jnp.int32)
    phase_turns = jnp.mod(frequency[:, None] * position[None, :], PIX).astype(jnp.float32)
    phase_angle = phase_turns * (2.0 * math.pi / PIX)
    cosine = jnp.cos(phase_angle)
    sine_table = jnp.sin(phase_angle)
    table_one = jnp.concatenate(
        [jnp.concatenate([cosine, sine_table], 1), jnp.concatenate([-sine_table, cosine], 1)], 0
    )
    table_two = jnp.concatenate(
        [
            jnp.concatenate([cosine.T, -sine_table.T], 1),
            jnp.concatenate([sine_table.T, cosine.T], 1),
        ],
        0,
    )
    return (table_one, table_two)


def pupil_mask(radius):
    frequency = jnp.arange(W, dtype=jnp.int32) - W // 2
    distance = frequency[:, None] * frequency[:, None] + frequency[None, :] * frequency[None, :]
    return (distance <= radius * radius).astype(jnp.bfloat16)


def source_power(window, table_one, table_two):
    tile_count = window.shape[0]
    split_parts = (
        window.reshape(tile_count, 6, 2, W, W)
        .transpose(0, 1, 3, 2, 4)
        .reshape(tile_count, 6, W, 2 * W)
    )
    half_field = jnp.einsum(
        "bcik,ky->bciy", split_parts.astype(jnp.float32), table_one, precision=lax.Precision.HIGHEST
    )
    half_field = (
        half_field.reshape(tile_count, 6, W, 2, PIX)
        .transpose(0, 1, 3, 2, 4)
        .reshape(tile_count, 6, 2 * W, PIX)
    )
    image_field = jnp.einsum(
        "pk,bcky->bcpy", table_two, half_field, precision=lax.Precision.HIGHEST
    )
    power_map = jnp.sum((image_field * image_field).reshape(tile_count, 12, PIX, PIX), axis=1)
    return power_map.reshape(tile_count, PIX * PIX)


def local(
    tile_tokens,
    norm_gain,
    up_weight,
    down_weight,
    head_weight,
    source_index,
    source_cutoff,
    source_weight,
):
    residual = tile_tokens.astype(jnp.float32)
    mean_square = jnp.mean(residual * residual, axis=1, keepdims=True)
    normed = (residual * lax.rsqrt(mean_square + 1e-05) * norm_gain).astype(jnp.bfloat16)
    token_count = tile_tokens.shape[0]
    columns = normed
    pre_act = jnp.dot(
        columns,
        lax.all_gather(up_weight, "tile", axis=0, tiled=True),
        preferred_element_type=jnp.float32,
    )
    hidden = jax.nn.gelu(pre_act).astype(jnp.bfloat16)
    columns = hidden
    branch_out = jnp.dot(
        columns,
        lax.all_gather(down_weight, "tile", axis=0, tiled=True),
        preferred_element_type=jnp.float32,
    )
    mixed = (residual + branch_out).astype(jnp.bfloat16)
    coeffs = jnp.dot(
        mixed,
        lax.all_gather(head_weight, "src", axis=1, tiled=True),
        preferred_element_type=jnp.float32,
    ).astype(jnp.bfloat16)
    tile_count = token_count // PATCH
    spectra = (
        coeffs.reshape(tile_count, GRID, GRID, 12, SUB, SUB)
        .transpose(0, 3, 1, 4, 2, 5)
        .reshape(tile_count, 12, ORD, ORD)
    )
    group_count = lax.axis_size("tile")
    my_group = lax.axis_index("tile")
    anchor_zero = jnp.zeros((), jnp.int32)
    local_weight = lax.dynamic_slice_in_dim(source_weight, my_group * SRC_DEV, SRC_DEV, 0)
    table_one, table_two = dft_tables()
    image_count = group_count * tile_count
    running = jnp.zeros((image_count, PIX * PIX), jnp.float32)
    corner = jnp.min(source_index.reshape(group_count, SRC_DEV, 2), axis=1)

    def cut_region(corner_at):
        return lax.dynamic_slice(
            spectra,
            (anchor_zero, anchor_zero, corner_at[0], corner_at[1]),
            (tile_count, 12, REG, REG),
        )

    cut_blocks = jax.vmap(cut_region)(corner).reshape(group_count, tile_count, 12, REG * REG)
    received = lax.all_to_all(cut_blocks, "tile", split_axis=0, concat_axis=1, tiled=True)
    region = received.reshape(image_count, 12, REG, REG)
    base_corner = lax.dynamic_index_in_dim(corner, my_group, 0, keepdims=False)
    local_index = (
        lax.dynamic_slice_in_dim(source_index, my_group * SRC_DEV, SRC_DEV, 0)
        - base_corner[None, :]
    )
    local_cutoff = lax.dynamic_slice_in_dim(source_cutoff, my_group * SRC_DEV, SRC_DEV, 0)

    def add_source(total, source_item):
        corner_at, radius, weight = source_item
        window = lax.dynamic_slice(
            region, (anchor_zero, anchor_zero, corner_at[0], corner_at[1]), (image_count, 12, W, W)
        ) * pupil_mask(radius)
        return (total + weight * source_power(window, table_one, table_two), None)

    image_sum, unused = lax.scan(add_source, running, (local_index, local_cutoff, local_weight))
    norm_scale = 1.0 / (6.0 * W * W * source_weight.shape[0])
    everything = lax.psum(image_sum, "tile")
    result = lax.dynamic_slice_in_dim(everything, my_group * tile_count, tile_count, 0)
    return result * norm_scale


def solution(mesh):
    return jax.shard_map(
        local,
        mesh=mesh,
        in_specs=(
            P(("tile", "src"), None),
            P(),
            P("tile", None),
            P("tile", None),
            P(None, "src"),
            P(),
            P(),
            P(),
        ),
        out_specs=P(("tile", "src"), None),
        check_vma=False,
    )
```

profile of v0, /device:TPU:0, one launch (start us, length us, event | category | flops | bytes accessed | tf_op | source)
XLA Modules:
  0.0 1103.8 jit_solution(1894265273519993116)
XLA Ops:
  11.3 174.9 %all-gather.4.cloned.1.call-done = bf16[2048,2816]{1,0:T(8,128)(2,1)} async-done(((bf16[64,2816]{1,0:T(8,128)(2,1)}), bf16[2048,2816]{1,0:T(8,128)(2,1)}) %all-gather.4.cloned.1.call-update) | async-done | bytes 11534352 | tf_op jit(solution)/shard_map/all_gather | solution.py:83
  186.2 174.7 %all-gather.6.cloned.1.call-done = bf16[2816,2048]{1,0:T(8,128)(2,1)} async-done(((bf16[88,2048]{1,0:T(8,128)(2,1)}), bf16[2816,2048]{1,0:T(8,128)(2,1)}) %all-gather.6.cloned.1.call-update) | async-done | bytes 11534352 | tf_op jit(solution)/shard_map/all_gather | solution.py:90
  360.9 14.3 %fusion.12 = bf16[256,2048]{1,0:T(8,128)(2,1)S(1)} fusion(bf16[2816,2048]{1,0:T(8,128)(2,1)} %all-gather.6.cloned.1.call-done, bf16[256,2048]{1,0:T(8,128)(2,1)} %param.10, bf16[2048,2816]{1,0:T(8,128)(2,1)} %all-gather.4.cloned.1.call-done, f32[2048]{0:T(1024)} %param.11, f32[256]{0:T(256)S(1)} %add_rsqrt_fusion), kind=kOutput, calls=%fused_computation.25 | convolution fusion | flops 5915738112 | bytes 25175040 | tf_op jit(solution)/shard_map/dot_general | solution.py:88
  375.2 18.3 %all-gather.8.cloned.1.call-done = bf16[2048,768]{0,1:T(8,128)(2,1)} async-done(((bf16[2048,192]{0,1:T(8,128)(2,1)}), bf16[2048,768]{0,1:T(8,128)(2,1)}) %all-gather.8.cloned.1.call-update) | async-done | bytes 3145744 | tf_op jit(solution)/shard_map/all_gather | solution.py:96
  393.5 2.9 convolution_convert_fusion
  396.6 2.1 reshape.116
  398.8 5.3 copy.23
  404.1 8.2 reshape.117
  412.3 87.3 %while.14 = (s32[]{:T(128)}, bf16[1,12,128,128]{3,2,1,0:T(8,128)(2,1)S(1)}, s32[32,4]{0,1:T(4,128)S(1)}, bf16[32,1,12,64,64]{4,3,2,1,0:T(8,128)(2,1)}, s32[]{:T(128)}) while((s32[]{:T(128)}, bf16[1,12,128,128]{3,2,1,0:T(8,128)(2,1)S(1)}, s32[32,4]{0,1:T(4,128)S(1)}, bf16[32,1,12,64,64]{4,3,2,1,0:T(8,128)(2,1)}, s32[]{:T(128)}) %tuple.54), condition=%wide.while_cond, body=%wide.while_body.sunk | while | flops 2 | bytes 296561 | solution.py:115
  418.4 2.1 bitcast_dynamic-update-slice_fusion.2
  437.5 2.1 bitcast_dynamic-update-slice_fusion.2
  453.9 2.1 bitcast_dynamic-update-slice_fusion.2
  475.7 2.1 bitcast_dynamic-update-slice_fusion.2
  494.8 2.1 bitcast_dynamic-update-slice_fusion.2
  499.6 9.7 reshape.154
  509.3 7.5 all-to-all-start
  518.0 53.1 %all-to-all-done = bf16[32,1,12,4096]{3,2,1,0:T(8,128)(2,1)} async-done(((bf16[32,1,12,4096]{3,2,1,0:T(8,128)(2,1)}), bf16[32,1,12,4096]{3,2,1,0:T(8,128)(2,1)}, u32[]{:S(2)}, u32[]{:S(2)}) %all-to-all-start) | async-done | bytes 3145760 | tf_op jit(solution)/shard_map/all_to_all | solution.py:122
  571.0 9.9 reshape.155
  581.0 206.1 %while.15 = (s32[]{:T(128)}, f32[32,4096]{1,0:T(8,128)}, f32[4]{0:T(128)S(1)}, s32[4,2]{0,1:T(2,128)S(1)}, bf16[32,12,64,64]{3,2,1,0:T(8,128)(2,1)}, /*index=5*/...) while((s32[]{:T(128)}, f32[32,4096]{1,0:T(8,128)}, ...), condition=%wide.region_4.5_spmd.clone, body=%wide.region_2.4_spmd.clone.sunk | while | flops 1816923136 | bytes 45421140 | solution.py:138
  587.2 4.7 dynamic-slice_multiply_fusion.3
  591.9 3.3 copy.38
  595.3 2.6 reshape.159
  597.9 4.1 fusion.74
  601.9 12.1 %multiply_bitcast_fusion.2 = f32[32,6,128,64]{2,3,1,0:T(8,128)} fusion(f32[32,6,64,64]{3,2,1,0:T(8,128)S(1)} %bitcast.81, f32[128,64]{0,1:T(8,128)S(1)} %get-tuple-element.322), kind=kOutput, calls=%fused_computation.2.clone.1 | convolution fusion | flops 1209532416 | bytes 9469952 | tf_op jit(solution)/shard_map/while/body/eval_jaxpr/pk,bcky->bcpy/dot_general | solution.py:59
  614.1 9.6 copy.39
  623.7 6.3 reduce_sum.25
  638.8 4.5 dynamic-slice_multiply_fusion.3
  643.3 3.3 copy.38
  646.6 2.6 reshape.159
  649.2 4.1 fusion.74
  653.3 12.1 %multiply_bitcast_fusion.2 = f32[32,6,128,64]{2,3,1,0:T(8,128)} fusion(f32[32,6,64,64]{3,2,1,0:T(8,128)S(1)} %bitcast.81, f32[128,64]{0,1:T(8,128)S(1)} %get-tuple-element.322), kind=kOutput, calls=%fused_computation.2.clone.1 | convolution fusion | flops 1209532416 | bytes 9469952 | tf_op jit(solution)/shard_map/while/body/eval_jaxpr/pk,bcky->bcpy/dot_general | solution.py:59
  665.5 9.6 copy.39
  675.0 6.3 reduce_sum.25
  690.1 4.7 dynamic-slice_multiply_fusion.3
  694.9 3.3 copy.38
  698.2 2.6 reshape.159
  700.8 4.1 fusion.74
  704.9 12.1 %multiply_bitcast_fusion.2 = f32[32,6,128,64]{2,3,1,0:T(8,128)} fusion(f32[32,6,64,64]{3,2,1,0:T(8,128)S(1)} %bitcast.81, f32[128,64]{0,1:T(8,128)S(1)} %get-tuple-element.322), kind=kOutput, calls=%fused_computation.2.clone.1 | convolution fusion | flops 1209532416 | bytes 9469952 | tf_op jit(solution)/shard_map/while/body/eval_jaxpr/pk,bcky->bcpy/dot_general | solution.py:59
  717.1 9.6 copy.39
  726.6 6.3 reduce_sum.25
  741.7 4.7 dynamic-slice_multiply_fusion.3
  746.5 3.3 copy.38
  749.8 2.6 reshape.159
  752.4 4.1 fusion.74
  756.5 12.1 %multiply_bitcast_fusion.2 = f32[32,6,128,64]{2,3,1,0:T(8,128)} fusion(f32[32,6,64,64]{3,2,1,0:T(8,128)S(1)} %bitcast.81, f32[128,64]{0,1:T(8,128)S(1)} %get-tuple-element.322), kind=kOutput, calls=%fused_computation.2.clone.1 | convolution fusion | flops 1209532416 | bytes 9469952 | tf_op jit(solution)/shard_map/while/body/eval_jaxpr/pk,bcky->bcpy/dot_general | solution.py:59
  768.6 9.6 copy.39
  778.2 6.3 reduce_sum.25
  787.1 308.6 %all-reduce.2.cloned.1.call-done = f32[32,4096]{1,0:T(8,128)} async-done(((f32[32,4096]{1,0:T(8,128)}), f32[32,4096]{1,0:T(8,128)}) %all-reduce.2.cloned.1.call-update) | async-done | bytes 524304 | tf_op jit(solution)/shard_map/psum | solution.py:140
  (179 shorter events, 99.9 us)
Async XLA Ops:
  6.5 179.7 %all-gather.4.cloned.1.call-start = ((), (), s32[]{:S(2)}) async-start(), calls=%async_computation.1 | async-start | bytes 11894784 | tf_op jit(solution)/shard_map/all_gather | solution.py:83
  7.3 353.7 %all-gather.6.cloned.1.call-start = ((), (), s32[]{:S(2)}) async-start(), calls=%async_computation.2 | async-start | bytes 11894784 | tf_op jit(solution)/shard_map/all_gather | solution.py:90
  8.0 385.5 %all-gather.8.cloned.1.call-start = ((), (), s32[]{:S(2)}) async-start(), calls=%async_computation.3 | async-start | bytes 3932160 | tf_op jit(solution)/shard_map/all_gather | solution.py:96
  509.3 7.8 copy-start.3
  509.3 7.9 copy-start.4
  509.3 8.5 copy-start.2
  509.3 61.7 %all-to-all-start = ((bf16[32,1,12,4096]{3,2,1,0:T(8,128)(2,1)}), bf16[32,1,12,4096]{3,2,1,0:T(8,128)(2,1)}, u32[]{:S(2)}, u32[]{:S(2)}) async-start(bf16[32,1,12,4096]{3,2,1,0:T(8,128)(2,1)} %bitcast.83), calls=%async_computation | async-start | bytes 8388608 | tf_op jit(solution)/shard_map/all_to_all | solution.py:122
  516.9 578.9 %all-reduce.2.cloned.1.call-start = ((), (), s32[]{:S(2)}) async-start(), calls=%async_computation.4 | async-start | bytes 1048576 | tf_op jit(solution)/shard_map/psum | solution.py:140
  629.9 1.7 copy-start
  631.7 0.8 copy-start.1
  681.3 1.7 copy-start
  683.1 0.8 copy-start.1
  732.9 1.7 copy-start
  734.7 0.8 copy-start.1
  784.5 1.7 copy-start
  786.3 0.8 copy-start.1
Sparse Core Ops, SparseCore 0:
  9.0 177.1 all-gather.3
  187.8 173.0 all-gather.5
  362.6 30.8 all-gather.7
  787.3 308.4 all-reduce.1
where the time goes:
time: 1110 us; the launch traced here: 1100 us
  waiting for transfers between devices  732 us (66%)
  local copies, waits for them, and re-layouts  198 us (18%)
  matrix products  82.1 us (7%)
  other arithmetic  51.2 us (5%)
  loops' own time  20 us (2%)
  between operations  13.3 us (1%)
    psum x1, waiting for transfers between devices, local(): everything = lax.psum(image_sum, 'tile')  309 us
    all_gather x1, waiting for transfers between devices, local(): lax.all_gather(up_weight, 'tile', axis=0, tiled=True)  175 us
    all_gather x1, waiting for transfers between devices, local(): lax.all_gather(down_weight, 'tile', axis=0, tiled=True)  175 us
    gather x96, local copies, waits for them, and re-layouts  87.2 us
    all_to_all x1, waiting for transfers between devices, local(): lax.all_to_all(cut_blocks, 'tile', split_axis=0, concat_axis=1, tiled=True)  53.1 us
    dot_general x4, matrix products, source_power(): jnp.einsum('pk,bcky->bcpy', table_two, half_field, precision=lax.Precisio...  48.6 us
    mul x4, local copies, waits for them, and re-layouts, source_power(): image_field * image_field  38.2 us
    reduce_sum x4, other arithmetic, source_power(): jnp.sum((image_field * image_field).reshape(tile_count, 12, PIX, PIX), ax...  25 us
  transfers between devices with their start and end apart: 5, of which 5 were waited for; matrix products, arithmetic and copies ran while one was open for 2% of the time, Pallas kernels for 0%

commit v1 on v0

v1 whole, which is shorter than its diff:
```python
import math

import jax
import jax.numpy as jnp
from jax import lax
from jax.sharding import PartitionSpec as P

GRID = 16
SUB = 8
W = 32
REG = 64
PIX = 64
SRC_DEV = 4
PATCH = 256
ORD = 128
f32 = jnp.float32
bf16 = jnp.bfloat16


def split_bf16(x):
    hi = lax.reduce_precision(x, exponent_bits=8, mantissa_bits=7)
    lo = x - hi
    return hi.astype(bf16), lo.astype(bf16)


def phase_tables():
    turn = 2.0 * math.pi / PIX
    v = jnp.arange(ORD, dtype=jnp.int32)
    y = jnp.arange(PIX, dtype=jnp.int32)
    ang = jnp.mod(v[:, None] * y[None, :], PIX).astype(f32) * turn
    cv, sv = jnp.cos(ang), jnp.sin(ang)
    t1 = jnp.stack([jnp.concatenate([cv, sv], 1), jnp.concatenate([-sv, cv], 1)], 0)
    i = jnp.arange(W, dtype=jnp.int32)
    x = jnp.arange(PIX, dtype=jnp.int32)
    ang2 = jnp.mod(x[:, None] * i[None, :], PIX).astype(f32) * turn
    ca, sa = jnp.cos(ang2), jnp.sin(ang2)
    t2 = jnp.stack([jnp.stack([ca, -sa], 1), jnp.stack([sa, ca], 1)], 0)
    return t1, t2


def imaging(spec, source_index, source_cutoff, source_weight):
    T = spec.shape[0]
    S = source_index.shape[0]
    x0 = jnp.clip(source_index[:, 0], 0, ORD - W)
    y0 = jnp.clip(source_index[:, 1], 0, ORD - W)
    rows = (x0[:, None] + jnp.arange(W, dtype=jnp.int32)[None, :]).reshape(-1)
    spec_rows = spec.reshape(T, 6, 2, ORD, ORD).transpose(3, 0, 1, 2, 4)
    strips = jnp.take(spec_rows, rows, axis=0, mode="clip").reshape(S, W, T, 6, 2, ORD)
    i = jnp.arange(W, dtype=jnp.int32)
    j = jnp.arange(ORD, dtype=jnp.int32)[None, :] - y0[:, None]
    dist = (i[None, :, None] - W // 2) ** 2 + (j[:, None, :] - W // 2) ** 2
    keep = (dist <= (source_cutoff * source_cutoff)[:, None, None]) & (j[:, None, :] >= 0) & (j[:, None, :] < W)
    masked = jnp.where(keep[:, :, None, None, None, :], strips, jnp.zeros((), bf16))
    t1, t2 = phase_tables()
    t1h, t1l = split_bf16(t1)
    t1s = jnp.concatenate([t1h, t1l], -1)
    out1 = jnp.einsum("sitkpv,pvn->sitkn", masked, t1s, preferred_element_type=f32)
    half = out1[..., : 2 * PIX] + out1[..., 2 * PIX:]
    half = half.reshape(S, W, T, 6, 2, PIX)
    hh, hl = split_bf16(half)
    hcat = jnp.concatenate([hh, hl, hh], 4)
    t2h, t2l = split_bf16(t2)
    t2cat = jnp.concatenate([t2h, t2h, t2l], 2)
    field = jnp.einsum("cxqi,sitkqy->tskcxy", t2cat, hcat, preferred_element_type=f32)
    power = jnp.sum(field * field * source_weight[None, :, None, None, None, None], axis=(1, 2, 3))
    return power.reshape(T, PIX * PIX) * (1.0 / (6.0 * W * W * S))


def local(
    tile_tokens,
    norm_gain,
    up_weight,
    down_weight,
    head_weight,
    source_index,
    source_cutoff,
    source_weight,
):
    residual = tile_tokens.astype(jnp.float32)
    mean_square = jnp.mean(residual * residual, axis=1, keepdims=True)
    normed = (residual * lax.rsqrt(mean_square + 1e-05) * norm_gain).astype(jnp.bfloat16)
    token_count = tile_tokens.shape[0]
    columns = normed
    pre_act = jnp.dot(
        columns,
        lax.all_gather(up_weight, "tile", axis=0, tiled=True),
        preferred_element_type=jnp.float32,
    )
    hidden = jax.nn.gelu(pre_act).astype(jnp.bfloat16)
    columns = hidden
    branch_out = jnp.dot(
        columns,
        lax.all_gather(down_weight, "tile", axis=0, tiled=True),
        preferred_element_type=jnp.float32,
    )
    mixed = (residual + branch_out).astype(jnp.bfloat16)
    coeffs = jnp.dot(
        mixed,
        lax.all_gather(head_weight, "src", axis=1, tiled=True),
        preferred_element_type=jnp.float32,
    ).astype(jnp.bfloat16)
    tile_count = token_count // PATCH
    spectra = (
        coeffs.reshape(tile_count, GRID, GRID, 12, SUB, SUB)
        .transpose(0, 3, 1, 4, 2, 5)
        .reshape(tile_count, 12, ORD, ORD)
    )
    return imaging(spectra, source_index, source_cutoff, source_weight)


def solution(mesh):
    return jax.shard_map(
        local,
        mesh=mesh,
        in_specs=(
            P(("tile", "src"), None),
            P(),
            P("tile", None),
            P("tile", None),
            P(None, "src"),
            P(),
            P(),
            P(),
        ),
        out_specs=P(("tile", "src"), None),
        check_vma=False,
    )
```

time: 1110 us -> 549 us (0.49)
  waiting for transfers between devices: 732 us -> 365 us
  local copies, waits for them, and re-layouts: 198 us -> 89.1 us
  matrix products: 82.1 us -> 38.7 us
  loops' own time: 20 us -> 0 us
    psum x1 -> x0, waiting for transfers between devices: 309 us -> none  [local(): everything = lax.psum(image_sum, 'tile')]
    all_to_all x1 -> x0, waiting for transfers between devices: 53.1 us -> none  [local(): lax.all_to_all(cut_blocks, 'tile', split_axis=0, concat_axis=1, tiled=True)]
    dot_general x8 -> x2, matrix products: 64.8 us -> 21.5 us  [the longest x1 12.1 us: imaging(): jnp.einsum('sitkpv,pvn->sitkn', masked, t1s, preferred_element_type=f32)]
    reshape x8 -> x0, local copies, waits for them, and re-layouts: 39.1 us -> none  [the longest x4 10.4 us: source_power(): split_parts = window.reshape(tile_count, 6, 2, W, W).transpose(0, 1, 3, 2...]
    mul x8 -> x2, local copies, waits for them, and re-layouts: 39.7 us -> 0.78 us  [imaging(): return power.reshape(T, PIX * PIX) * (1.0 / (6.0 * W * W * S))]
    gather x96 -> x2, local copies, waits for them, and re-layouts: 87.2 us -> 59.1 us  [imaging(): jnp.take(spec_rows, rows, axis=0, mode='clip').reshape(S, W, T, 6, 2, ORD)]
    reduce_sum x4 -> x0, other arithmetic: 25 us -> none  [source_power(): jnp.sum((image_field * image_field).reshape(tile_count, 12, PIX, PIX), ax...]
    mul x13 -> x2, other arithmetic: 23 us -> 0.74 us  [the longest x1 0.73 us: imaging(): source_cutoff * source_cutoff]
  transfers between devices with their start and end apart: 5 -> 3, of which waited for: 5 -> 3; matrix products, arithmetic and copies ran while one was open for 2% -> 4% of each run, Pallas kernels for 0% -> 0%
where the time goes in v1:
time: 549 us; the launch traced here: 548 us
  waiting for transfers between devices  365 us (66%)
  local copies, waits for them, and re-layouts  89.1 us (16%)
  other arithmetic  42.1 us (8%)
  matrix products  38.7 us (7%)
  between operations  13.3 us (2%)
    all_gather x1, waiting for transfers between devices, local(): lax.all_gather(down_weight, 'tile', axis=0, tiled=True)  175 us
    all_gather x1, waiting for transfers between devices, local(): lax.all_gather(up_weight, 'tile', axis=0, tiled=True)  169 us
    gather x2, local copies, waits for them, and re-layouts, imaging(): jnp.take(spec_rows, rows, axis=0, mode='clip').reshape(S, W, T, 6, 2, ORD)  59.1 us
    convert_element_type x3, other arithmetic, split_bf16(): return (hi.astype(bf16), lo.astype(bf16))  18.7 us
    all_gather x1, waiting for transfers between devices, local(): lax.all_gather(head_weight, 'src', axis=1, tiled=True)  18.3 us
    add x1, other arithmetic, imaging(): half = out1[..., :2 * PIX] + out1[..., 2 * PIX:]  14.5 us
    dot_general x1, matrix products, local(): jnp.dot(columns, lax.all_gather(down_weight, 'tile', axis=0, tiled=True),...  14.3 us
    another operation x2, local copies, waits for them, and re-layouts, imaging(): spec_rows = spec.reshape(T, 6, 2, ORD, ORD).transpose(3, 0, 1, 2, 4)  14.1 us
  transfers between devices with their start and end apart: 3, of which 3 were waited for; matrix products, arithmetic and copies ran while one was open for 4% of the time, Pallas kernels for 0%

profile of v1, /device:TPU:0, one launch (start us, length us, event | category | flops | bytes accessed | tf_op | source)
XLA Modules:
  0.0 547.8 jit_solution(6147798405518693012)
XLA Ops:
  6.5 0.0 all-gather.4.cloned.1.call-start
  6.5 0.7 all-gather.4.cloned.1.call-update
  7.3 0.0 all-gather.6.cloned.1.call-start
  7.3 0.7 all-gather.6.cloned.1.call-update
  8.0 0.0 all-gather.8.cloned.1.call-start
  8.1 0.7 all-gather.8.cloned.1.call-update
  8.7 0.7 mul.195
  9.5 0.8 clamp_bitcast_fusion.1
  10.2 0.1 iota_add_fusion
  10.3 0.1 reshape.264
  10.4 0.1 fusion.66
  10.5 0.1 fusion.64
  10.6 0.3 fusion.57
  10.9 0.6 reduce-precision_convert_fusion.2
  11.5 0.3 fusion.55
  11.8 0.1 maximum_bitcast_fusion.8
  11.9 0.7 reduce-precision_convert_fusion.1
  12.6 1.5 fusion.21
  14.1 0.1 fusion.53
  14.2 0.1 add_multiply_fusion
  14.3 2.4 fusion.25
  16.7 169.5 %all-gather.4.cloned.1.call-done = bf16[2048,2816]{1,0:T(8,128)(2,1)} async-done(((bf16[64,2816]{1,0:T(8,128)(2,1)}), bf16[2048,2816]{1,0:T(8,128)(2,1)}) %all-gather.4.cloned.1.call-update) | async-done | bytes 11534352 | tf_op jit(solution)/shard_map/all_gather | solution.py:86
  186.2 174.7 %all-gather.6.cloned.1.call-done = bf16[2816,2048]{1,0:T(8,128)(2,1)} async-done(((bf16[88,2048]{1,0:T(8,128)(2,1)}), bf16[2816,2048]{1,0:T(8,128)(2,1)}) %all-gather.6.cloned.1.call-update) | async-done | bytes 11534352 | tf_op jit(solution)/shard_map/all_gather | solution.py:93
  360.9 14.3 %fusion.20 = bf16[256,2048]{1,0:T(8,128)(2,1)S(1)} fusion(bf16[2816,2048]{1,0:T(8,128)(2,1)} %all-gather.6.cloned.1.call-done, bf16[256,2048]{1,0:T(8,128)(2,1)} %param.8, bf16[2048,2816]{1,0:T(8,128)(2,1)} %all-gather.4.cloned.1.call-done, f32[2048]{0:T(1024)} %param.9, f32[256]{0:T(256)S(1)} %add_rsqrt_fusion), kind=kOutput, calls=%fused_computation.30 | convolution fusion | flops 5915738112 | bytes 25175040 | tf_op jit(solution)/shard_map/dot_general | solution.py:91
  375.2 18.3 %all-gather.8.cloned.1.call-done = bf16[2048,768]{0,1:T(8,128)(2,1)} async-done(((bf16[2048,192]{0,1:T(8,128)(2,1)}), bf16[2048,768]{0,1:T(8,128)(2,1)}) %all-gather.8.cloned.1.call-update) | async-done | bytes 3145744 | tf_op jit(solution)/shard_map/all_gather | solution.py:99
  393.5 2.9 convolution_convert_fusion
  396.4 0.2 copy.27
  396.6 2.3 reshape.256
  398.9 5.4 copy.41
  404.3 8.7 %reshape.277 = bf16[1,6,2,128,128]{4,2,1,3,0:T(2,128)(2,1)S(1)} reshape(bf16[1,12,16,8,16,8]{5,4,1,3,2,0:T(8,128)(2,1)} %copy.41) | data formatting | bytes 786432 | tf_op jit(solution)/shard_map/reshape;reshape | solution.py:47
  413.0 51.6 %gather_fusion = bf16[4096,6,2,128]{3,2,1,0:T(2,128)(2,1)} fusion(bf16[128,6,2,128]{3,2,1,0:T(2,128)(2,1)S(1)} %bitcast.61, s32[4096]{0:T(1024)S(1)} %broadcast_clamp_fusion), kind=kCustom, calls=%fused_computation | custom fusion | bytes 25182208 | tf_op jit(solution)/shard_map/jit(_take)/gather | solution.py:48
  464.7 7.4 %copy.30 = bf16[4096,6,2,128]{3,0,2,1:T(8,128)(2,1)S(1)} copy(bf16[4096,6,2,128]{3,2,1,0:T(2,128)(2,1)} %gather_fusion) | data formatting | bytes 25165824 | tf_op jit(solution)/shard_map/jit(_take)/gather | solution.py:48
  472.1 0.0 copy-done
  472.1 0.0 copy-start.1
  472.1 0.0 copy-start.2
  472.1 2.5 broadcast_select_fusion
  474.6 0.0 copy-done.1
  474.6 0.0 copy-done.2
  474.6 12.1 %fusion.9 = f32[128,32,1,6,256]{4,0,3,1,2:T(8,128)} fusion(bf16[128,32,6,2,128]{4,1,0,3,2:T(8,128)(2,1)S(1)} %broadcast_select_fusion, bf16[2,128,128]{2,1,0:T(8,128)(2,1)S(1)} %copy-done.2, bf16[2,128,128]{2,1,0:T(8,128)(2,1)S(1)} %copy-done.1), kind=kOutput, calls=%fused_computation.17 | convolution fusion | flops 3221487616 | bytes 37879808 | tf_op jit(solution)/shard_map/sitkpv,pvn->sitkn/dot_general | solution.py:57
  486.7 14.5 %slice_add_fusion = f32[128,32,1,6,128]{4,0,3,1,2:T(8,128)} fusion(f32[128,32,1,6,256]{4,0,3,1,2:T(8,128)} %fusion.9), kind=kLoop, calls=%fused_computation.13 | loop fusion | flops 3145728 | bytes 37748736 | tf_op jit(solution)/shard_map/add | solution.py:58
  501.2 12.6 %copy.32 = f32[128,32,1,6,128]{0,4,3,1,2:T(8,128)} copy(f32[128,32,1,6,128]{4,0,3,1,2:T(8,128)} %slice_add_fusion) | data formatting | bytes 25165824 | tf_op jit(solution)/shard_map/add | solution.py:58
  513.8 17.3 %fusion.6 = (bf16[128,32,1,6,2,64]{0,1,4,5,3,2:T(8,128)(2,1)}, bf16[128,32,1,6,2,64]{0,1,4,5,3,2:T(8,128)(2,1)}) fusion(f32[128,32,1,6,2,64]{0,5,4,3,1,2:T(8,128)} %bitcast.62), kind=kLoop, calls=%fused_computation.12 | loop fusion | flops 12582912 | bytes 25165824 | tf_op jit(solution)/shard_map/convert_element_type | solution.py:23
  531.2 0.0 copy-done.3
  531.2 0.0 copy-done.4
  531.2 0.0 copy-done.5
  531.2 9.3 %fusion = f32[64,64]{1,0:T(8,128)S(1)} fusion(f32[128]{0:T(128)S(1)} %copy-done.5, bf16[128,32,1,6,2,64]{0,1,4,5,3,2:T(8,128)(2,1)} %get-tuple-element.6, bf16[128,32,1,6,2,64]{0,1,4,5,3,2:T(8,128)(2,1)} %get-tuple-element.5, bf16[2,64,2,32]{1,3,2,0:T(8,128)(2,1)S(1)} %copy-done.4, bf16[2,64,2,32]{1,3,2,0:T(8,128)(2,1)S(1)} %copy-done.3), kind=kOutput, calls=%fused_computation.2 | convolution fusion | flops 2491559936 | bytes 12632576 | tf_op jit(solution)/shard_map/cxqi,sitkqy->tskcxy/dot_general | solution.py:64
  540.5 0.1 copy.35
  540.6 0.7 mul.225
  (9 shorter events, 0.0 us)
Async XLA Ops:
  6.5 179.7 %all-gather.4.cloned.1.call-start = ((), (), s32[]{:S(2)}) async-start(), calls=%async_computation | async-start | bytes 11894784 | tf_op jit(solution)/shard_map/all_gather | solution.py:86
  7.3 353.7 %all-gather.6.cloned.1.call-start = ((), (), s32[]{:S(2)}) async-start(), calls=%async_computation.1 | async-start | bytes 11894784 | tf_op jit(solution)/shard_map/all_gather | solution.py:93
  8.0 385.5 %all-gather.8.cloned.1.call-start = ((), (), s32[]{:S(2)}) async-start(), calls=%async_computation.2 | async-start | bytes 3932160 | tf_op jit(solution)/shard_map/all_gather | solution.py:99
  464.7 7.4 %copy-start = (pred[128,32,128]{2,1,0:T(8,128)(4,1)S(1)}, pred[128,32,128]{2,1,0:T(8,128)(4,1)}, u32[]{:S(2)}) copy-start(pred[128,32,128]{2,1,0:T(8,128)(4,1)} %fusion.25) | copy-start | bytes 1572868
  472.1 2.5 copy-start.1
  472.1 2.5 copy-start.2
  513.8 17.4 %copy-start.3 = (bf16[2,64,2,32]{1,3,2,0:T(8,128)(2,1)S(1)}, bf16[2,64,2,32]{1,3,2,0:T(8,128)(2,1)}, u32[]{:S(2)}) copy-start(bf16[2,64,2,32]{1,3,2,0:T(8,128)(2,1)} %get-tuple-element.9) | copy-start | bytes 49156
  513.8 17.4 %copy-start.4 = (bf16[2,64,2,32]{1,3,2,0:T(8,128)(2,1)S(1)}, bf16[2,64,2,32]{1,3,2,0:T(8,128)(2,1)}, u32[]{:S(2)}) copy-start(bf16[2,64,2,32]{1,3,2,0:T(8,128)(2,1)} %get-tuple-element.10) | copy-start | bytes 49156
  513.8 17.4 %copy-start.5 = (f32[128]{0:T(128)S(1)}, f32[128]{0:T(128)}, u32[]{:S(2)}) copy-start(f32[128]{0:T(128)} %param.15) | copy-start | bytes 1540
Sparse Core Ops, SparseCore 0:
  9.0 177.1 all-gather.3
  187.8 173.0 all-gather.5
  362.6 30.8 all-gather.7
